TPU v7x, 128 devices: a whole 4x4x4 slice. The times are simulated.
128 devices in a mesh: grp: 4 (over y), tile: 32 (over x, z, core).
Axes of the slice: x: 4, y: 4, z: 4, core: 2. Of those that a mesh axis runs over, the one named last changes fastest.
Arguments:
- amp_tiles: bfloat16 [65536, 64, 64], P(('grp', 'tile')), may hold values from -6 to 6
- amp_row: int32 [65536], P(('grp', 'tile')), may hold values from 0 to 1024, as said below
- amp_col: int32 [65536], P(('grp', 'tile')), may hold values from 0 to 61
- cycle_panel: bfloat16 [3968, 3968], P('grp'), may hold values from -0.09375 to 0.09375
Outputs:
- residual: bfloat16 [65536, 64, 64], P(('grp', 'tile'))
Inputs may be any that keep to these rules, and one draw needn't show every extreme that they name: `amp_row`: tiles n of block k = n // 512 lie in group h = k // 32: their rows are h * 256 to (h + 1) * 256 - 1, or 1024 for an empty slot. No two non-empty tiles name the same row and column tile. Within one block of 512 tiles at most 16 name rows of one run r * 8 to (r + 1) * 8 - 1, and 16 is reached in every draw; in every group some run has all its 496 tiles present.
All inputs are finite; a program needn't handle non-finite values.
Results may differ from a plain program's by a relative error of at most 0.001.
Values may be sent and summed in bfloat16 or wider, within the bound.
No kernel may reach another device: no remote copies, remote signals or barrier semaphores. Data moves between devices by JAX's collectives and lax.ppermute only.
A program may use at most 192 MiB of HBM per device.

v0:
```python
import jax
import jax.numpy as jnp
from jax import lax
from jax.sharding import PartitionSpec as P

ROWT_DEV = 8


def pick_rows(index, count, data):
    onehot = (index[None, :] == jnp.arange(count)[:, None]).astype(data.dtype)
    return jnp.dot(onehot, data, preferred_element_type=jnp.float32).astype(data.dtype)


def take_rows(index, data):
    onehot = (index[:, None] == jnp.arange(data.shape[0])[None, :]).astype(data.dtype)
    return jnp.dot(onehot, data, preferred_element_type=jnp.float32).astype(data.dtype)


def to_blocks(out, edge):
    rows, cols = out.shape
    return (
        out.reshape(rows // edge, edge, cols // edge, edge)
        .transpose(0, 2, 1, 3)
        .reshape(rows // edge * (cols // edge), edge * edge)
    )


def layer(amp_tiles, amp_row, amp_col, cycle_panel):
    parts = lax.axis_size("tile")
    count = amp_tiles.shape[0]
    capacity = count // parts
    edge = amp_tiles.shape[1]
    width = cycle_panel.shape[1]
    nvt = width // edge
    per_dest = ROWT_DEV * nvt
    group_rows = ROWT_DEV * parts
    first = lax.axis_index("grp") * group_rows
    local_row = amp_row - first
    live = local_row < group_rows
    target = jnp.where(live, local_row // ROWT_DEV, parts)
    onehot = (target[:, None] == jnp.arange(parts)[None, :]).astype(jnp.int32)
    rank = jnp.sum(jnp.cumsum(onehot, axis=0) * onehot, axis=1) - 1
    position = jnp.where(live, target * capacity + rank, parts * capacity)
    block_id = local_row % ROWT_DEV * nvt + amp_col
    flat = amp_tiles.reshape(count, edge * edge)
    send_tiles = pick_rows(position, parts * capacity, flat)
    send_ids = (
        jnp.full((parts * capacity,), per_dest, jnp.int32).at[position].set(block_id, mode="drop")
    )
    recv_tiles, recv_ids = (
        lax.all_to_all(send_tiles, "tile", split_axis=0, concat_axis=0, tiled=True),
        lax.all_to_all(send_ids, "tile", split_axis=0, concat_axis=0, tiled=True),
    )
    dense = pick_rows(recv_ids, per_dest, recv_tiles)
    dense = (
        dense.reshape(ROWT_DEV, nvt, edge, edge)
        .transpose(0, 2, 1, 3)
        .reshape(ROWT_DEV * edge, width)
    )
    core = lax.axis_index("tile") % 2
    span = (width // 2 + 127) // 128 * 128
    shift = (width - span) // edge
    mine = lax.dynamic_slice_in_dim(cycle_panel, core * (width - span), span, axis=1)
    gathered = lax.all_gather(mine, "grp", axis=0, tiled=True)
    partner = lax.ppermute(gathered, "tile", [(i, i ^ 1) for i in range(parts)])
    half = span // edge
    valid = recv_ids < per_dest
    row_t = recv_ids // nvt
    col_t = recv_ids % nvt
    col_mine = col_t - core * shift
    in_mine = valid & (col_mine >= 0) & (col_mine < half)
    col_partner = col_t - (1 - core) * shift
    in_partner = valid & ~in_mine
    idx_mine = jnp.where(in_mine, row_t * half + col_mine, ROWT_DEV * half)
    idx_partner = jnp.where(in_partner, row_t * half + col_partner, ROWT_DEV * half)
    out_mine = jnp.dot(dense, gathered, preferred_element_type=jnp.float32).astype(jnp.bfloat16)
    ans_mine = take_rows(idx_mine, to_blocks(out_mine, edge))
    out_partner = jnp.dot(dense, partner, preferred_element_type=jnp.float32).astype(jnp.bfloat16)
    ans_partner = take_rows(idx_partner, to_blocks(out_partner, edge))
    answer = ans_mine + ans_partner
    returned = lax.all_to_all(answer, "tile", split_axis=0, concat_axis=0, tiled=True)
    onehot_back = (position[None, :] == jnp.arange(parts * capacity)[:, None]).astype(returned.dtype)
    result_t = jnp.dot(returned.T, onehot_back, preferred_element_type=jnp.float32).astype(returned.dtype)
    return result_t.T.reshape(count, edge, edge)


def solution(mesh):
    in_specs = (
        P(("grp", "tile"), None, None),
        P(("grp", "tile")),
        P(("grp", "tile")),
        P("grp", None),
    )
    out_specs = P(("grp", "tile"), None, None)
    return jax.shard_map(layer, mesh=mesh, in_specs=in_specs, out_specs=out_specs, check_vma=False)
```

profile of v0, /device:TPU:1, one launch (start us, length us, event | category | flops | bytes accessed | tf_op | source)
XLA Modules:
  0.0 434.7 jit_solution(4056304333115449456)
XLA Ops:
  6.5 0.0 all-gather.2.cloned.1.call-start
  6.5 0.0 copy-start
  6.5 0.0 copy-start.1
  6.5 4.7 %constant_dynamic-slice_fusion = bf16[992,2048]{1,0:T(8,128)(2,1)} fusion(bf16[992,3968]{1,0:T(8,128)(2,1)} %param.7, s32[]{:T(128)S(6)} %select_n.75), kind=kLoop, calls=%fused_computation.55 | loop fusion | bytes 8126468 | tf_op jit(solution)/shard_map/dynamic_slice | solution.py:63
  11.2 0.0 all-gather.2.cloned.1.call-update
  11.3 152.8 %all-gather.2.cloned.1.call-done = bf16[3968,2048]{1,0:T(8,128)(2,1)} async-done(((bf16[992,2048]{1,0:T(8,128)(2,1)}), bf16[3968,2048]{1,0:T(8,128)(2,1)}) %all-gather.2.cloned.1.call-update) | async-done | bytes 16252944 | tf_op jit(solution)/shard_map/all_gather | solution.py:64
  164.0 0.8 collective-permute-start
  164.9 0.0 copy-done
  164.9 0.0 copy-done.1
  164.9 1.2 reduce-window.6
  166.1 0.2 slice_reduce_fusion
  166.4 0.1 fusion.7
  166.5 2.4 scatter_custom_fusion
  168.9 0.7 all_to_all.24
  169.6 7.1 %all-to-all-start = ((s32[32,16,1]{1,2,0:T(1,128)}), s32[32,16,1]{1,2,0:T(1,128)S(1)}, u32[]{:S(2)}, u32[]{:S(2)}) async-start(s32[32,16,1]{1,2,0:T(1,128)} %bitcast.2), calls=%async_computation | async-start | bytes 32768 | tf_op jit(solution)/shard_map/all_to_all | solution.py:52
  176.7 6.6 %convolution_convert_fusion.3 = bf16[512,4096]{1,0:T(8,128)(2,1)} fusion(bf16[512,4096]{0,1:T(8,128)(2,1)} %bitcast.55, s32[512]{0:T(512)S(1)} %get-tuple-element.6), kind=kOutput, calls=%fused_computation.4 | convolution fusion | flops 2149842944 | bytes 8390656 | tf_op jit(solution)/shard_map/dot_general | solution.py:11
  183.3 6.0 %all-to-all-done = s32[32,16,1]{1,2,0:T(1,128)S(1)} async-done(((s32[32,16,1]{1,2,0:T(1,128)}), s32[32,16,1]{1,2,0:T(1,128)S(1)}, u32[]{:S(2)}, u32[]{:S(2)}) %all-to-all-start) | async-done | bytes 2080 | tf_op jit(solution)/shard_map/all_to_all | solution.py:52
  189.3 7.4 %all-to-all-start.1 = ((bf16[32,16,4096]{2,1,0:T(8,128)(2,1)}), bf16[32,16,4096]{2,1,0:T(8,128)(2,1)}, u32[]{:S(2)}, u32[]{:S(2)}) async-start(bf16[32,16,4096]{2,1,0:T(8,128)(2,1)} %bitcast.52), calls=%async_computation.1 | async-start | bytes 8388608 | tf_op jit(solution)/shard_map/all_to_all | solution.py:51
  196.7 0.5 broadcast.188
  197.3 0.7 reduce.5
  197.9 0.1 all_to_all.26
  198.0 50.8 %all-to-all-done.1 = bf16[32,16,4096]{2,1,0:T(8,128)(2,1)} async-done(((bf16[32,16,4096]{2,1,0:T(8,128)(2,1)}), bf16[32,16,4096]{2,1,0:T(8,128)(2,1)}, u32[]{:S(2)}, u32[]{:S(2)}) %all-to-all-start.1) | async-done | bytes 4194336 | tf_op jit(solution)/shard_map/all_to_all | solution.py:51
  248.8 6.4 %convolution_convert_fusion.4 = bf16[496,4096]{1,0:T(8,128)(2,1)} fusion(bf16[512,4096]{1,0:T(8,128)(2,1)} %bitcast.5, s32[512]{0:T(512)S(1)} %all_to_all.26), kind=kOutput, calls=%fused_computation.5 | convolution fusion | flops 2082660352 | bytes 8259584 | tf_op jit(solution)/shard_map/dot_general | solution.py:11
  255.2 12.1 %reshape.99 = bf16[8,62,64,64]{3,2,1,0:T(8,128)(2,1)} reshape(bf16[496,4096]{1,0:T(8,128)(2,1)} %convolution_convert_fusion.4) | data formatting | bytes 8126464 | tf_op jit(solution)/shard_map/reshape | solution.py:56
  267.3 12.1 %copy.13 = bf16[8,62,64,64]{2,0,3,1:T(8,128)(2,1)} copy(bf16[8,62,64,64]{3,2,1,0:T(8,128)(2,1)} %reshape.99) | data formatting | bytes 8126464 | tf_op jit(solution)/shard_map/reshape | solution.py:56
  279.4 11.5 %reshape.100 = bf16[512,3968]{0,1:T(8,128)(2,1)} reshape(bf16[8,64,62,64]{1,0,3,2:T(8,128)(2,1)} %bitcast.48) | data formatting | bytes 8126464 | tf_op jit(solution)/shard_map/reshape | solution.py:58
  290.9 13.5 %convolution_convert_fusion.6 = bf16[512,2048]{1,0:T(8,128)(2,1)S(1)} fusion(bf16[512,3968]{0,1:T(8,128)(2,1)} %reshape.100, bf16[3968,2048]{1,0:T(8,128)(2,1)} %all-gather.2.cloned.1.call-done), kind=kOutput, calls=%fused_computation.10 | convolution fusion | flops 8322547712 | bytes 22413312 | tf_op jit(solution)/shard_map/dot_general | solution.py:76
  304.4 5.3 %reshape.101 = bf16[8,64,32,64]{3,2,1,0:T(8,128)(2,1)} reshape(bf16[512,2048]{1,0:T(8,128)(2,1)S(1)} %convolution_convert_fusion.6) | data formatting | bytes 4194304 | tf_op jit(solution)/shard_map/reshape | solution.py:22
  309.8 5.8 %copy.22 = bf16[8,64,32,64]{3,1,2,0:T(8,128)(2,1)} copy(bf16[8,64,32,64]{3,2,1,0:T(8,128)(2,1)} %reshape.101) | data formatting | bytes 4194304 | tf_op jit(solution)/shard_map/reshape | solution.py:22
  315.5 5.7 %reshape.102 = bf16[256,4096]{1,0:T(8,128)(2,1)S(1)} reshape(bf16[8,32,64,64]{3,2,1,0:T(8,128)(2,1)} %bitcast.50) | data formatting | bytes 4194304 | tf_op jit(solution)/shard_map/reshape | solution.py:24
  321.2 0.0 collective-permute-done
  321.2 14.7 %convolution_convert_fusion.5 = bf16[512,2048]{1,0:T(8,128)(2,1)} fusion(bf16[512,3968]{0,1:T(8,128)(2,1)} %reshape.100, bf16[3968,2048]{1,0:T(8,128)(2,1)} %collective-permute-done), kind=kOutput, calls=%fused_computation.9 | convolution fusion | flops 8322547712 | bytes 22413312 | tf_op jit(solution)/shard_map/dot_general | solution.py:78
  335.9 7.1 %reshape.103 = bf16[8,64,32,64]{3,2,1,0:T(8,128)(2,1)} reshape(bf16[512,2048]{1,0:T(8,128)(2,1)} %convolution_convert_fusion.5) | data formatting | bytes 4194304 | tf_op jit(solution)/shard_map/reshape | solution.py:22
  343.0 5.7 %copy.21 = bf16[8,64,32,64]{3,1,2,0:T(8,128)(2,1)} copy(bf16[8,64,32,64]{3,2,1,0:T(8,128)(2,1)} %reshape.103) | data formatting | bytes 4194304 | tf_op jit(solution)/shard_map/reshape | solution.py:22
  348.8 6.6 %reshape.104 = bf16[256,4096]{1,0:T(8,128)(2,1)} reshape(bf16[8,32,64,64]{3,2,1,0:T(8,128)(2,1)} %bitcast.51) | data formatting | bytes 4194304 | tf_op jit(solution)/shard_map/reshape | solution.py:24
  355.4 2.9 convolution_convert_fusion.1
  358.3 1.4 fusion
  359.6 57.4 %all_to_all.36 = bf16[32,16,4096]{2,1,0:T(8,128)(2,1)S(1)} all-to-all(bf16[32,16,4096]{2,1,0:T(8,128)(2,1)S(1)} %bitcast.49), channel_id=1, replica_groups=mesh['grp'=4,'tile'=32] {'tile'}, dimensions={0} | all-to-all | bytes 8388608 | tf_op jit(solution)/shard_map/all_to_all | solution.py:81
  417.1 4.3 convolution_convert_fusion
  421.4 6.4 %copy.16 = bf16[512,4096]{0,1:T(8,128)(2,1)} copy(bf16[512,4096]{1,0:T(8,128)(2,1)} %convolution_convert_fusion) | data formatting | bytes 8388608 | tf_op jit(solution)/shard_map/convert_element_type | solution.py:83
  (6 shorter events, 0.1 us)
Async XLA Ops:
  6.5 157.5 %all-gather.2.cloned.1.call-start = ((), (), s32[]{:S(2)}) async-start(), calls=%async_computation.3 | async-start | bytes 20316160 | tf_op jit(solution)/shard_map/all_gather | solution.py:64
  6.5 158.4 %copy-start = (s32[512]{0:T(512)S(1)}, s32[512]{0:T(512)}, u32[]{:S(2)}) copy-start(s32[512]{0:T(512)} %param.5) | copy-start | bytes 6148
  6.5 158.4 %copy-start.1 = (s32[512]{0:T(512)S(1)}, s32[512]{0:T(512)}, u32[]{:S(2)}) copy-start(s32[512]{0:T(512)} %param.6) | copy-start | bytes 6148
  164.0 157.2 %collective-permute-start = (bf16[3968,2048]{1,0:T(8,128)(2,1)}, bf16[3968,2048]{1,0:T(8,128)(2,1)}, u32[]{:S(2)}, u32[]{:S(2)}) collective-permute-start(bf16[3968,2048]{1,0:T(8,128)(2,1)} %all-gather.2.cloned.1.call-done), channel_id=1, source_target_pairs={{0,1},{1,0},{2,3},{3,2},{4,5},{5,4},{6,7},{7,6},{8,9},{9,8},{10,11... | collective-permute-start | bytes 48758792 | tf_op jit(solution)/shard_map/ppermute | solution.py:65
  169.6 19.7 %all-to-all-start = ((s32[32,16,1]{1,2,0:T(1,128)}), s32[32,16,1]{1,2,0:T(1,128)S(1)}, u32[]{:S(2)}, u32[]{:S(2)}) async-start(s32[32,16,1]{1,2,0:T(1,128)} %bitcast.2), calls=%async_computation | async-start | bytes 32768 | tf_op jit(solution)/shard_map/all_to_all | solution.py:52
  189.3 59.5 %all-to-all-start.1 = ((bf16[32,16,4096]{2,1,0:T(8,128)(2,1)}), bf16[32,16,4096]{2,1,0:T(8,128)(2,1)}, u32[]{:S(2)}, u32[]{:S(2)}) async-start(bf16[32,16,4096]{2,1,0:T(8,128)(2,1)} %bitcast.52), calls=%async_computation.1 | async-start | bytes 8388608 | tf_op jit(solution)/shard_map/all_to_all | solution.py:51
Sparse Core Ops, SparseCore 0:
  11.4 152.6 all-gather.1
where the time goes:
time: 436 us; the launch traced here: 435 us
  waiting for transfers between devices  210 us (48%)
  local copies, waits for them, and re-layouts  86.9 us (20%)
  blocking collectives  57.4 us (13%)
  matrix products  49.8 us (11%)
  starting transfers between devices  15.4 us (4%)
  between operations  13.5 us (3%)
    all_gather x1, waiting for transfers between devices, layer(): gathered = lax.all_gather(mine, 'grp', axis=0, tiled=True)  153 us
    all_to_all x1, blocking collectives, layer(): lax.all_to_all(answer, 'tile', split_axis=0, concat_axis=0, tiled=True)  57.4 us
    all_to_all x1, waiting for transfers between devices, layer(): lax.all_to_all(send_tiles, 'tile', split_axis=0, concat_axis=0, tiled=True)  50.8 us
    reshape x2, local copies, waits for them, and re-layouts, layer(): dense.reshape(ROWT_DEV, nvt, edge, edge).transpose(0, 2, 1, 3)  24.2 us
    reshape x4, local copies, waits for them, and re-layouts, to_blocks(): out.reshape(rows // edge, edge, cols // edge, edge).transpose(0, 2, 1, 3)  23.9 us
    dot_general x1, matrix products, layer(): jnp.dot(dense, partner, preferred_element_type=jnp.float32)  14.7 us
    dot_general x1, matrix products, layer(): jnp.dot(dense, gathered, preferred_element_type=jnp.float32)  13.5 us
    dot_general x2, matrix products, pick_rows(): jnp.dot(onehot, data, preferred_element_type=jnp.float32).astype(data.dtype)  13 us
  transfers between devices with their start and end apart: 4, of which 3 were waited for; matrix products, arithmetic and copies ran while one was open for 19% of the time, Pallas kernels for 0%

commit v1 on v0

--- a/solution.py
+++ b/solution.py
@@ -2,8 +2,11 @@
 import jax.numpy as jnp
 from jax import lax
 from jax.sharding import PartitionSpec as P
+from jax.experimental import pallas as pl
+from jax.experimental.pallas import tpu as pltpu
 
 ROWT_DEV = 8
+CHUNKS = 4
 
 
 def pick_rows(index, count, data):
@@ -16,13 +19,43 @@
     return jnp.dot(onehot, data, preferred_element_type=jnp.float32).astype(data.dtype)
 
 
-def to_blocks(out, edge):
-    rows, cols = out.shape
-    return (
-        out.reshape(rows // edge, edge, cols // edge, edge)
-        .transpose(0, 2, 1, 3)
-        .reshape(rows // edge * (cols // edge), edge * edge)
-    )
+def tiles_to_rows(tiles, row_tiles, edge):
+    col_tiles = tiles.shape[0] // row_tiles
+
+    def kernel(x_ref, o_ref):
+        for r in range(row_tiles):
+            x = x_ref[r * col_tiles : (r + 1) * col_tiles, :]
+            x = jnp.swapaxes(x.reshape(col_tiles, edge, edge), 0, 1)
+            o_ref[r * edge : (r + 1) * edge, :] = x.reshape(edge, col_tiles * edge)
+
+    nbytes = tiles.size * tiles.dtype.itemsize
+    return pl.pallas_call(
+        kernel,
+        out_shape=jax.ShapeDtypeStruct((row_tiles * edge, col_tiles * edge), tiles.dtype),
+        in_specs=[pl.BlockSpec(memory_space=pltpu.VMEM)],
+        out_specs=pl.BlockSpec(memory_space=pltpu.VMEM),
+        cost_estimate=pl.CostEstimate(flops=0, transcendentals=0, bytes_accessed=2 * nbytes),
+    )(tiles)
+
+
+def rows_to_tiles(rows, edge):
+    row_tiles = rows.shape[0] // edge
+    col_tiles = rows.shape[1] // edge
+
+    def kernel(x_ref, o_ref):
+        for r in range(row_tiles):
+            x = x_ref[r * edge : (r + 1) * edge, :]
+            x = jnp.swapaxes(x.reshape(edge, col_tiles, edge), 0, 1)
+            o_ref[r * col_tiles : (r + 1) * col_tiles, :] = x.reshape(col_tiles, edge * edge)
+
+    nbytes = rows.size * rows.dtype.itemsize
+    return pl.pallas_call(
+        kernel,
+        out_shape=jax.ShapeDtypeStruct((row_tiles * col_tiles, edge * edge), rows.dtype),
+        in_specs=[pl.BlockSpec(memory_space=pltpu.VMEM)],
+        out_specs=pl.BlockSpec(memory_space=pltpu.VMEM),
+        cost_estimate=pl.CostEstimate(flops=0, transcendentals=0, bytes_accessed=2 * nbytes),
+    )(rows)
 
 
 def layer(amp_tiles, amp_row, amp_col, cycle_panel):
@@ -51,19 +84,12 @@
         lax.all_to_all(send_tiles, "tile", split_axis=0, concat_axis=0, tiled=True),
         lax.all_to_all(send_ids, "tile", split_axis=0, concat_axis=0, tiled=True),
     )
-    dense = pick_rows(recv_ids, per_dest, recv_tiles)
-    dense = (
-        dense.reshape(ROWT_DEV, nvt, edge, edge)
-        .transpose(0, 2, 1, 3)
-        .reshape(ROWT_DEV * edge, width)
-    )
+    dense = tiles_to_rows(pick_rows(recv_ids, per_dest, recv_tiles), ROWT_DEV, edge)
     core = lax.axis_index("tile") % 2
     span = (width // 2 + 127) // 128 * 128
     shift = (width - span) // edge
-    mine = lax.dynamic_slice_in_dim(cycle_panel, core * (width - span), span, axis=1)
-    gathered = lax.all_gather(mine, "grp", axis=0, tiled=True)
-    partner = lax.ppermute(gathered, "tile", [(i, i ^ 1) for i in range(parts)])
     half = span // edge
+    chunk = half // CHUNKS
     valid = recv_ids < per_dest
     row_t = recv_ids // nvt
     col_t = recv_ids % nvt
@@ -71,13 +97,25 @@
     in_mine = valid & (col_mine >= 0) & (col_mine < half)
     col_partner = col_t - (1 - core) * shift
     in_partner = valid & ~in_mine
-    idx_mine = jnp.where(in_mine, row_t * half + col_mine, ROWT_DEV * half)
-    idx_partner = jnp.where(in_partner, row_t * half + col_partner, ROWT_DEV * half)
-    out_mine = jnp.dot(dense, gathered, preferred_element_type=jnp.float32).astype(jnp.bfloat16)
-    ans_mine = take_rows(idx_mine, to_blocks(out_mine, edge))
-    out_partner = jnp.dot(dense, partner, preferred_element_type=jnp.float32).astype(jnp.bfloat16)
-    ans_partner = take_rows(idx_partner, to_blocks(out_partner, edge))
-    answer = ans_mine + ans_partner
+    unused = ROWT_DEV * chunk
+    pieces = []
+    for q in range(CHUNKS):
+        mine = lax.dynamic_slice_in_dim(
+            cycle_panel, core * (width - span) + q * chunk * edge, chunk * edge, axis=1
+        )
+        gathered = lax.all_gather(mine, "grp", axis=0, tiled=True)
+        partner = lax.ppermute(gathered, "tile", [(i, i ^ 1) for i in range(parts)])
+        lm = col_mine - q * chunk
+        idx_mine = jnp.where(in_mine & (lm >= 0) & (lm < chunk), row_t * chunk + lm, unused)
+        lp = col_partner - q * chunk
+        idx_partner = jnp.where(in_partner & (lp >= 0) & (lp < chunk), row_t * chunk + lp, unused)
+        out_mine = jnp.dot(dense, gathered, preferred_element_type=jnp.float32).astype(jnp.bfloat16)
+        pieces.append(take_rows(idx_mine, rows_to_tiles(out_mine, edge)))
+        out_partner = jnp.dot(dense, partner, preferred_element_type=jnp.float32).astype(jnp.bfloat16)
+        pieces.append(take_rows(idx_partner, rows_to_tiles(out_partner, edge)))
+    answer = pieces[0]
+    for piece in pieces[1:]:
+        answer = answer + piece
     returned = lax.all_to_all(answer, "tile", split_axis=0, concat_axis=0, tiled=True)
     onehot_back = (position[None, :] == jnp.arange(parts * capacity)[:, None]).astype(returned.dtype)
     result_t = jnp.dot(returned.T, onehot_back, preferred_element_type=jnp.float32).astype(returned.dtype)

time: 436 us -> 365 us (0.84)
  local copies, waits for them, and re-layouts: 86.9 us -> 14.6 us
  waiting for transfers between devices: 210 us -> 140 us
  Pallas kernels: 0 us -> 31.6 us
  matrix products: 49.8 us -> 79.8 us
  starting transfers between devices: 15.4 us -> 20.5 us
    reshape x9 -> x0, local copies, waits for them, and re-layouts: 71.9 us -> none  [the longest x2 24.2 us: layer(): dense.reshape(ROWT_DEV, nvt, edge, edge).transpose(0, 2, 1, 3)]
    all_to_all x1, waiting for transfers between devices: 50.8 us -> 0.01 us  [layer(): lax.all_to_all(send_tiles, 'tile', split_axis=0, concat_axis=0, tiled=True)]
    pallas_call x0 -> x9, Pallas kernels: none -> 31.6 us  [the longest x8 22.4 us: rows_to_tiles(): pl.pallas_call(kernel, out_shape=jax.ShapeDtypeStruct((row_tiles * col_ti...]
    all_gather x1 -> x4, waiting for transfers between devices: 153 us -> 138 us  [layer(): gathered = lax.all_gather(mine, 'grp', axis=0, tiled=True)]
    dot_general x1 -> x4, matrix products: 13.5 us -> 26 us  [layer(): jnp.dot(dense, gathered, preferred_element_type=jnp.float32)]
    dot_general x1 -> x4, matrix products: 14.7 us -> 26.1 us  [layer(): jnp.dot(dense, partner, preferred_element_type=jnp.float32)]
    dot_general x2 -> x8, matrix products: 4.27 us -> 10.3 us  [take_rows(): jnp.dot(onehot, data, preferred_element_type=jnp.float32).astype(data.dtype)]
    all_to_all x1, waiting for transfers between devices: 5.96 us -> 0.4 us  [layer(): lax.all_to_all(send_ids, 'tile', split_axis=0, concat_axis=0, tiled=True)]
  transfers between devices with their start and end apart: 4 -> 10, of which waited for: 3 -> 5; matrix products, arithmetic and copies ran while one was open for 19% -> 18% of each run, Pallas kernels for 0% -> 8%
where the time goes in v1:
time: 365 us; the launch traced here: 360 us
  waiting for transfers between devices  140 us (38%)
  matrix products  79.8 us (22%)
  blocking collectives  57.5 us (16%)
  Pallas kernels  31.6 us (9%)
  starting transfers between devices  20.5 us (6%)
  local copies, waits for them, and re-layouts  14.6 us (4%)
  between operations  13.6 us (4%)
    all_gather x4, waiting for transfers between devices, layer(): gathered = lax.all_gather(mine, 'grp', axis=0, tiled=True)  138 us
    all_to_all x1, blocking collectives, layer(): lax.all_to_all(answer, 'tile', split_axis=0, concat_axis=0, tiled=True)  57.5 us
    dot_general x4, matrix products, layer(): jnp.dot(dense, partner, preferred_element_type=jnp.float32)  26.1 us
    dot_general x4, matrix products, layer(): jnp.dot(dense, gathered, preferred_element_type=jnp.float32)  26 us
    pallas_call x8, Pallas kernels, rows_to_tiles(): pl.pallas_call(kernel, out_shape=jax.ShapeDtypeStruct((row_tiles * col_ti...  22.4 us
    dot_general x2, matrix products, pick_rows(): jnp.dot(onehot, data, preferred_element_type=jnp.float32).astype(data.dtype)  13 us
    dot_general x8, matrix products, take_rows(): jnp.dot(onehot, data, preferred_element_type=jnp.float32).astype(data.dtype)  10.3 us
    all_to_all x1, starting transfers between devices, layer(): lax.all_to_all(send_ids, 'tile', split_axis=0, concat_axis=0, tiled=True)  9.42 us
  transfers between devices with their start and end apart: 10, of which 5 were waited for; matrix products, arithmetic and copies ran while one was open for 18% of the time, Pallas kernels for 8%

profile of v1, /device:TPU:1, one launch (start us, length us, event | category | flops | bytes accessed | tf_op | source)
XLA Modules:
  0.0 360.0 jit_solution(5251835056590644524)
XLA Ops:
  6.5 4.2 %constant_dynamic-slice_fusion = (bf16[992,512]{1,0:T(8,128)(2,1)}, bf16[992,512]{1,0:T(8,128)(2,1)}, bf16[992,512]{1,0:T(8,128)(2,1)}, bf16[992,512]{1,0:T(8,128)(2,1)}) fusion(bf16[992,3968]{1,0:T(8,128)(2,1)} %param.7, s32[]{:T(128)S(6)} %select_n.171, s32[]{:T(128)S(6)} %select_n.165, s32[]{:T(128)S(6)} %select_n.162, s32[]{:T(128)S(6)} %select_n.168), kind=kLoop, calls=%fused_computation.92 | loop fusion | bytes 8126480 | tf_op jit(solution)/shard_map/dynamic_slice | solution.py:103
  10.8 0.7 all-gather.7.cloned.1.call-update
  11.5 0.7 all-gather.9.cloned.1.call-update
  12.9 1.2 reduce-window.6
  14.4 2.4 scatter_custom_fusion
  16.9 0.7 all_to_all.24
  17.5 9.4 %all-to-all-start = ((s32[32,16,1]{1,2,0:T(1,128)}), s32[32,16,1]{1,2,0:T(1,128)S(1)}, u32[]{:S(2)}, u32[]{:S(2)}) async-start(s32[32,16,1]{1,2,0:T(1,128)} %bitcast.2), calls=%async_computation | async-start | bytes 32768 | tf_op jit(solution)/shard_map/all_to_all | solution.py:85
  27.0 6.6 %convolution_convert_fusion.9 = bf16[512,4096]{1,0:T(8,128)(2,1)} fusion(bf16[512,4096]{0,1:T(8,128)(2,1)} %bitcast.55, s32[512]{0:T(512)S(1)} %get-tuple-element.10), kind=kOutput, calls=%fused_computation.10 | convolution fusion | flops 2149842944 | bytes 8390656 | tf_op jit(solution)/shard_map/dot_general | solution.py:14
  33.9 7.0 %all-to-all-start.1 = ((bf16[32,16,4096]{2,1,0:T(8,128)(2,1)}), bf16[32,16,4096]{2,1,0:T(8,128)(2,1)}, u32[]{:S(2)}, u32[]{:S(2)}) async-start(bf16[32,16,4096]{2,1,0:T(8,128)(2,1)} %bitcast.52), calls=%async_computation.1 | async-start | bytes 8388608 | tf_op jit(solution)/shard_map/all_to_all | solution.py:84
  41.0 20.1 %all-gather.5.cloned.1.call-done = bf16[3968,512]{1,0:T(8,128)(2,1)} async-done(((bf16[992,512]{1,0:T(8,128)(2,1)}), bf16[3968,512]{1,0:T(8,128)(2,1)}) %all-gather.5.cloned.1.call-update) | async-done | bytes 4063248 | tf_op jit(solution)/shard_map/all_gather | solution.py:106
  61.0 0.8 collective-permute-start
  61.9 0.6 broadcast.572
  62.5 0.7 reduce.5
  63.3 46.8 %all-gather.7.cloned.1.call-done = bf16[3968,512]{1,0:T(8,128)(2,1)} async-done(((bf16[992,512]{1,0:T(8,128)(2,1)}), bf16[3968,512]{1,0:T(8,128)(2,1)}) %all-gather.7.cloned.1.call-update) | async-done | bytes 4063248 | tf_op jit(solution)/shard_map/all_gather | solution.py:106
  110.2 1.3 collective-permute-start.1
  111.5 6.4 %convolution_convert_fusion.10.x_ref = bf16[496,4096]{1,0:T(8,128)(2,1)} fusion(bf16[512,4096]{1,0:T(8,128)(2,1)} %bitcast.5, s32[512]{0:T(512)S(1)} %all_to_all.26), kind=kOutput, calls=%fused_computation.11 | convolution fusion | flops 2082660352 | bytes 8259584 | tf_op jit(solution)/shard_map/dot_general | solution.py:14
  117.9 9.2 %shard_map.46 = bf16[512,3968]{1,0:T(8,128)(2,1)} custom-call(bf16[496,4096]{1,0:T(8,128)(2,1)} %convolution_convert_fusion.10.x_ref), custom_call_target="tpu_custom_call" | custom-call | bytes 8126464 | tf_op jit(solution)/shard_map/pallas_call | solution.py:32
  127.1 32.2 %all-gather.9.cloned.1.call-done = bf16[3968,512]{1,0:T(8,128)(2,1)} async-done(((bf16[992,512]{1,0:T(8,128)(2,1)}), bf16[3968,512]{1,0:T(8,128)(2,1)}) %all-gather.9.cloned.1.call-update) | async-done | bytes 4063248 | tf_op jit(solution)/shard_map/all_gather | solution.py:106
  159.3 0.8 collective-permute-start.2
  160.1 6.5 %convolution_convert_fusion.18.x_ref = bf16[512,512]{1,0:T(8,128)(2,1)} fusion(bf16[512,3968]{1,0:T(8,128)(2,1)} %shard_map.46, bf16[3968,512]{1,0:T(8,128)(2,1)} %all-gather.5.cloned.1.call-done), kind=kOutput, calls=%fused_computation.26 | convolution fusion | flops 2080636928 | bytes 8650752 | tf_op jit(solution)/shard_map/dot_general | solution.py:112
  166.6 2.8 shard_map.47
  169.4 38.9 %all-gather.11.cloned.1.call-done = bf16[3968,512]{1,0:T(8,128)(2,1)} async-done(((bf16[992,512]{1,0:T(8,128)(2,1)}), bf16[3968,512]{1,0:T(8,128)(2,1)}) %all-gather.11.cloned.1.call-update) | async-done | bytes 4063248 | tf_op jit(solution)/shard_map/all_gather | solution.py:106
  208.3 1.0 collective-permute-start.3
  209.3 6.5 %convolution_convert_fusion.16.x_ref = bf16[512,512]{1,0:T(8,128)(2,1)} fusion(bf16[512,3968]{1,0:T(8,128)(2,1)} %shard_map.46, bf16[3968,512]{1,0:T(8,128)(2,1)} %all-gather.7.cloned.1.call-done), kind=kOutput, calls=%fused_computation.24 | convolution fusion | flops 2080636928 | bytes 8650752 | tf_op jit(solution)/shard_map/dot_general | solution.py:112
  215.8 2.8 shard_map.49
  218.6 6.5 %convolution_convert_fusion.14.x_ref = bf16[512,512]{1,0:T(8,128)(2,1)} fusion(bf16[512,3968]{1,0:T(8,128)(2,1)} %shard_map.46, bf16[3968,512]{1,0:T(8,128)(2,1)} %all-gather.9.cloned.1.call-done), kind=kOutput, calls=%fused_computation.22 | convolution fusion | flops 2080636928 | bytes 8650752 | tf_op jit(solution)/shard_map/dot_general | solution.py:112
  225.1 2.7 shard_map.51
  227.8 6.5 %convolution_convert_fusion.12.x_ref = bf16[512,512]{1,0:T(8,128)(2,1)} fusion(bf16[512,3968]{1,0:T(8,128)(2,1)} %shard_map.46, bf16[3968,512]{1,0:T(8,128)(2,1)} %all-gather.11.cloned.1.call-done), kind=kOutput, calls=%fused_computation.20 | convolution fusion | flops 2080636928 | bytes 8650752 | tf_op jit(solution)/shard_map/dot_general | solution.py:112
  234.3 2.8 shard_map.53
  237.1 6.5 %convolution_convert_fusion.17.x_ref = bf16[512,512]{1,0:T(8,128)(2,1)} fusion(bf16[512,3968]{1,0:T(8,128)(2,1)} %shard_map.46, bf16[3968,512]{1,0:T(8,128)(2,1)} %collective-permute-done), kind=kOutput, calls=%fused_computation.25 | convolution fusion | flops 2080636928 | bytes 8650752 | tf_op jit(solution)/shard_map/dot_general | solution.py:114
  243.6 2.8 shard_map.48
  246.4 6.5 %convolution_convert_fusion.15.x_ref = bf16[512,512]{1,0:T(8,128)(2,1)} fusion(bf16[512,3968]{1,0:T(8,128)(2,1)} %shard_map.46, bf16[3968,512]{1,0:T(8,128)(2,1)} %collective-permute-done.1), kind=kOutput, calls=%fused_computation.23 | convolution fusion | flops 2080636928 | bytes 8650752 | tf_op jit(solution)/shard_map/dot_general | solution.py:114
  252.9 2.8 shard_map.50
  255.7 6.5 %convolution_convert_fusion.13.x_ref = bf16[512,512]{1,0:T(8,128)(2,1)} fusion(bf16[512,3968]{1,0:T(8,128)(2,1)} %shard_map.46, bf16[3968,512]{1,0:T(8,128)(2,1)} %collective-permute-done.2), kind=kOutput, calls=%fused_computation.21 | convolution fusion | flops 2080636928 | bytes 8650752 | tf_op jit(solution)/shard_map/dot_general | solution.py:114
  262.2 2.7 shard_map.52
  264.9 6.5 %convolution_convert_fusion.11.x_ref = bf16[512,512]{1,0:T(8,128)(2,1)} fusion(bf16[512,3968]{1,0:T(8,128)(2,1)} %shard_map.46, bf16[3968,512]{1,0:T(8,128)(2,1)} %collective-permute-done.3), kind=kOutput, calls=%fused_computation.19 | convolution fusion | flops 2080636928 | bytes 8650752 | tf_op jit(solution)/shard_map/dot_general | solution.py:114
  271.5 3.0 shard_map.54
  274.5 1.3 convolution_convert_fusion.7
  275.8 1.3 fusion
  277.1 1.3 fusion.1
  278.4 1.3 fusion.2
  279.8 1.3 fusion.3
  281.1 1.3 fusion.4
  282.4 1.3 fusion.5
  283.7 1.3 fusion.6
  285.0 57.5 %all_to_all.36 = bf16[32,16,4096]{2,1,0:T(8,128)(2,1)S(1)} all-to-all(bf16[32,16,4096]{2,1,0:T(8,128)(2,1)S(1)} %bitcast.51), channel_id=1, replica_groups=mesh['grp'=4,'tile'=32] {'tile'}, dimensions={0} | all-to-all | bytes 8388608 | tf_op jit(solution)/shard_map/all_to_all | solution.py:119
  342.5 4.4 %convolution_convert_fusion = bf16[512,4096]{1,0:T(8,128)(2,1)} fusion(bf16[512,4096]{1,0:T(8,128)(2,1)S(1)} %bitcast.53, s32[512]{0:T(512)S(1)} %get-tuple-element.10), kind=kOutput, calls=%fused_computation.1 | convolution fusion | flops 2149842944 | bytes 8390656 | tf_op jit(solution)/shard_map/dot_general | solution.py:121
  346.9 6.4 %copy.10 = bf16[512,4096]{0,1:T(8,128)(2,1)} copy(bf16[512,4096]{1,0:T(8,128)(2,1)} %convolution_convert_fusion) | data formatting | bytes 8388608 | tf_op jit(solution)/shard_map/convert_element_type | solution.py:121
  (42 shorter events, 1.7 us)
Async XLA Ops:
  6.5 54.5 %all-gather.5.cloned.1.call-start = ((), (), s32[]{:S(2)}) async-start(), calls=%async_computation.3 | async-start | bytes 5079040 | tf_op jit(solution)/shard_map/all_gather | solution.py:106
  6.5 6.3 %copy-start.8 = (s32[512]{0:T(512)S(1)}, s32[512]{0:T(512)}, u32[]{:S(2)}) copy-start(s32[512]{0:T(512)} %param.5) | copy-start | bytes 6148
  6.5 6.3 %copy-start.9 = (s32[512]{0:T(512)S(1)}, s32[512]{0:T(512)}, u32[]{:S(2)}) copy-start(s32[512]{0:T(512)} %param.6) | copy-start | bytes 6148
  10.7 99.4 %all-gather.7.cloned.1.call-start = ((), (), s32[]{:S(2)}) async-start(), calls=%async_computation.4 | async-start | bytes 5079040 | tf_op jit(solution)/shard_map/all_gather | solution.py:106
  11.5 147.8 %all-gather.9.cloned.1.call-start = ((), (), s32[]{:S(2)}) async-start(), calls=%async_computation.5 | async-start | bytes 5079040 | tf_op jit(solution)/shard_map/all_gather | solution.py:106
  12.2 196.1 %all-gather.11.cloned.1.call-start = ((), (), s32[]{:S(2)}) async-start(), calls=%async_computation.6 | async-start | bytes 5079040 | tf_op jit(solution)/shard_map/all_gather | solution.py:106
  17.5 16.4 %all-to-all-start = ((s32[32,16,1]{1,2,0:T(1,128)}), s32[32,16,1]{1,2,0:T(1,128)S(1)}, u32[]{:S(2)}, u32[]{:S(2)}) async-start(s32[32,16,1]{1,2,0:T(1,128)} %bitcast.2), calls=%async_computation | async-start | bytes 32768 | tf_op jit(solution)/shard_map/all_to_all | solution.py:85
  33.9 77.5 %all-to-all-start.1 = ((bf16[32,16,4096]{2,1,0:T(8,128)(2,1)}), bf16[32,16,4096]{2,1,0:T(8,128)(2,1)}, u32[]{:S(2)}, u32[]{:S(2)}) async-start(bf16[32,16,4096]{2,1,0:T(8,128)(2,1)} %bitcast.52), calls=%async_computation.1 | async-start | bytes 8388608 | tf_op jit(solution)/shard_map/all_to_all | solution.py:84
  61.0 176.0 %collective-permute-start = (bf16[3968,512]{1,0:T(8,128)(2,1)}, bf16[3968,512]{1,0:T(8,128)(2,1)}, u32[]{:S(2)}, u32[]{:S(2)}) collective-permute-start(bf16[3968,512]{1,0:T(8,128)(2,1)} %all-gather.5.cloned.1.call-done), channel_id=1, source_target_pairs={{0,1},{1,0},{2,3},{3,2},{4,5},{5,4},{6,7},{7,6},{8,9},{9,8},{10,11... | collective-permute-start | bytes 12189704 | tf_op jit(solution)/shard_map/ppermute | solution.py:107
  110.2 136.2 %collective-permute-start.1 = (bf16[3968,512]{1,0:T(8,128)(2,1)}, bf16[3968,512]{1,0:T(8,128)(2,1)}, u32[]{:S(2)}, u32[]{:S(2)}) collective-permute-start(bf16[3968,512]{1,0:T(8,128)(2,1)} %all-gather.7.cloned.1.call-done), channel_id=1, source_target_pairs={{0,1},{1,0},{2,3},{3,2},{4,5},{5,4},{6,7},{7,6},{8,9},{9,8},{10,11... | collective-permute-start | bytes 12189704 | tf_op jit(solution)/shard_map/ppermute | solution.py:107
  159.3 96.4 %collective-permute-start.2 = (bf16[3968,512]{1,0:T(8,128)(2,1)}, bf16[3968,512]{1,0:T(8,128)(2,1)}, u32[]{:S(2)}, u32[]{:S(2)}) collective-permute-start(bf16[3968,512]{1,0:T(8,128)(2,1)} %all-gather.9.cloned.1.call-done), channel_id=1, source_target_pairs={{0,1},{1,0},{2,3},{3,2},{4,5},{5,4},{6,7},{7,6},{8,9},{9,8},{10,11... | collective-permute-start | bytes 12189704 | tf_op jit(solution)/shard_map/ppermute | solution.py:107
  208.3 56.6 %collective-permute-start.3 = (bf16[3968,512]{1,0:T(8,128)(2,1)}, bf16[3968,512]{1,0:T(8,128)(2,1)}, u32[]{:S(2)}, u32[]{:S(2)}) collective-permute-start(bf16[3968,512]{1,0:T(8,128)(2,1)} %all-gather.11.cloned.1.call-done), channel_id=1, source_target_pairs={{0,1},{1,0},{2,3},{3,2},{4,5},{5,4},{6,7},{7,6},{8,9},{9,8},{10,11... | collective-permute-start | bytes 12189704 | tf_op jit(solution)/shard_map/ppermute | solution.py:107
  264.9 9.6 %copy-start.7 = (bf16[64,4096]{1,0:T(8,128)(2,1)S(1)}, bf16[64,4096]{1,0:T(8,128)(2,1)}, u32[]{:S(2)}) copy-start(bf16[64,4096]{1,0:T(8,128)(2,1)} %shard_map.48) | copy-start | bytes 1572868
  271.5 4.3 %copy-start.1 = (bf16[64,4096]{1,0:T(8,128)(2,1)S(1)}, bf16[64,4096]{1,0:T(8,128)(2,1)}, u32[]{:S(2)}) copy-start(bf16[64,4096]{1,0:T(8,128)(2,1)} %shard_map.47) | copy-start | bytes 1572868
  275.8 1.3 copy-start.3
  277.1 1.3 copy-start.5
  278.4 1.3 copy-start.2
  279.7 1.3 copy-start.6
  281.1 1.3 copy-start
  282.4 1.3 copy-start.4
Sparse Core Ops, SparseCore 0:
  10.8 50.1 all-gather.4
  62.7 47.4 all-gather.6
  111.8 47.4 all-gather.8
  160.8 47.4 all-gather.10

commit v2 on v1

--- a/solution.py
+++ b/solution.py
@@ -6,7 +6,6 @@
 from jax.experimental.pallas import tpu as pltpu
 
 ROWT_DEV = 8
-CHUNKS = 4
 
 
 def pick_rows(index, count, data):
@@ -88,8 +87,10 @@
     core = lax.axis_index("tile") % 2
     span = (width // 2 + 127) // 128 * 128
     shift = (width - span) // edge
+    mine = lax.dynamic_slice_in_dim(cycle_panel, core * (width - span), span, axis=1)
+    gathered = lax.all_gather(mine, "grp", axis=0, tiled=True)
+    partner = lax.ppermute(gathered, "tile", [(i, i ^ 1) for i in range(parts)])
     half = span // edge
-    chunk = half // CHUNKS
     valid = recv_ids < per_dest
     row_t = recv_ids // nvt
     col_t = recv_ids % nvt
@@ -97,25 +98,13 @@
     in_mine = valid & (col_mine >= 0) & (col_mine < half)
     col_partner = col_t - (1 - core) * shift
     in_partner = valid & ~in_mine
-    unused = ROWT_DEV * chunk
-    pieces = []
-    for q in range(CHUNKS):
-        mine = lax.dynamic_slice_in_dim(
-            cycle_panel, core * (width - span) + q * chunk * edge, chunk * edge, axis=1
-        )
-        gathered = lax.all_gather(mine, "grp", axis=0, tiled=True)
-        partner = lax.ppermute(gathered, "tile", [(i, i ^ 1) for i in range(parts)])
-        lm = col_mine - q * chunk
-        idx_mine = jnp.where(in_mine & (lm >= 0) & (lm < chunk), row_t * chunk + lm, unused)
-        lp = col_partner - q * chunk
-        idx_partner = jnp.where(in_partner & (lp >= 0) & (lp < chunk), row_t * chunk + lp, unused)
-        out_mine = jnp.dot(dense, gathered, preferred_element_type=jnp.float32).astype(jnp.bfloat16)
-        pieces.append(take_rows(idx_mine, rows_to_tiles(out_mine, edge)))
-        out_partner = jnp.dot(dense, partner, preferred_element_type=jnp.float32).astype(jnp.bfloat16)
-        pieces.append(take_rows(idx_partner, rows_to_tiles(out_partner, edge)))
-    answer = pieces[0]
-    for piece in pieces[1:]:
-        answer = answer + piece
+    idx_mine = jnp.where(in_mine, row_t * half + col_mine, ROWT_DEV * half)
+    idx_partner = jnp.where(in_partner, row_t * half + col_partner, ROWT_DEV * half)
+    out_mine = jnp.dot(dense, gathered, preferred_element_type=jnp.float32).astype(jnp.bfloat16)
+    ans_mine = take_rows(idx_mine, rows_to_tiles(out_mine, edge))
+    out_partner = jnp.dot(dense, partner, preferred_element_type=jnp.float32).astype(jnp.bfloat16)
+    ans_partner = take_rows(idx_partner, rows_to_tiles(out_partner, edge))
+    answer = ans_mine + ans_partner
     returned = lax.all_to_all(answer, "tile", split_axis=0, concat_axis=0, tiled=True)
     onehot_back = (position[None, :] == jnp.arange(parts * capacity)[:, None]).astype(returned.dtype)
     result_t = jnp.dot(returned.T, onehot_back, preferred_element_type=jnp.float32).astype(returned.dtype)

time: 365 us -> 383 us (1.049); the launches traced: 360 us -> 382 us
  waiting for transfers between devices: 140 us -> 210 us
  matrix products: 79.8 us -> 50.6 us
  Pallas kernels: 31.6 us -> 18.6 us
  starting transfers between devices: 20.5 us -> 15.4 us
    all_to_all x1, waiting for transfers between devices: 0.01 us -> 50.8 us  [layer(): lax.all_to_all(send_tiles, 'tile', split_axis=0, concat_axis=0, tiled=True)]
    all_gather x4 -> x1, waiting for transfers between devices: 138 us -> 153 us  [layer(): gathered = lax.all_gather(mine, 'grp', axis=0, tiled=True)]
    pallas_call x8 -> x2, Pallas kernels: 22.4 us -> 9.39 us  [rows_to_tiles(): pl.pallas_call(kernel, out_shape=jax.ShapeDtypeStruct((row_tiles * col_ti...]
    dot_general x4 -> x1, matrix products: 26.1 us -> 14.4 us  [layer(): jnp.dot(dense, partner, preferred_element_type=jnp.float32)]
    dot_general x4 -> x1, matrix products: 26 us -> 14.4 us  [layer(): jnp.dot(dense, gathered, preferred_element_type=jnp.float32)]
    dot_general x8 -> x2, matrix products: 10.3 us -> 4.4 us  [take_rows(): jnp.dot(onehot, data, preferred_element_type=jnp.float32).astype(data.dtype)]
    all_to_all x1, waiting for transfers between devices: 0.4 us -> 5.96 us  [layer(): lax.all_to_all(send_ids, 'tile', split_axis=0, concat_axis=0, tiled=True)]
  transfers between devices with their start and end apart: 10 -> 4, of which waited for: 5 -> 3; matrix products, arithmetic and copies ran while one was open for 18% -> 9% of each run, Pallas kernels for 8% -> 4%
where the time goes in v2:
time: 383 us; the launch traced here: 382 us
  waiting for transfers between devices  210 us (55%)
  blocking collectives  57.4 us (15%)
  matrix products  50.6 us (13%)
  Pallas kernels  18.6 us (5%)
  starting transfers between devices  15.4 us (4%)
  local copies, waits for them, and re-layouts  15.1 us (4%)
  between operations  13.5 us (4%)
    all_gather x1, waiting for transfers between devices, layer(): gathered = lax.all_gather(mine, 'grp', axis=0, tiled=True)  153 us
    all_to_all x1, blocking collectives, layer(): lax.all_to_all(answer, 'tile', split_axis=0, concat_axis=0, tiled=True)  57.4 us
    all_to_all x1, waiting for transfers between devices, layer(): lax.all_to_all(send_tiles, 'tile', split_axis=0, concat_axis=0, tiled=True)  50.8 us
    dot_general x1, matrix products, layer(): jnp.dot(dense, gathered, preferred_element_type=jnp.float32)  14.4 us
    dot_general x1, matrix products, layer(): jnp.dot(dense, partner, preferred_element_type=jnp.float32)  14.4 us
    dot_general x2, matrix products, pick_rows(): jnp.dot(onehot, data, preferred_element_type=jnp.float32).astype(data.dtype)  13 us
    pallas_call x2, Pallas kernels, rows_to_tiles(): pl.pallas_call(kernel, out_shape=jax.ShapeDtypeStruct((row_tiles * col_ti...  9.39 us
    pallas_call x1, Pallas kernels, tiles_to_rows(): pl.pallas_call(kernel, out_shape=jax.ShapeDtypeStruct((row_tiles * edge,...  9.22 us
  transfers between devices with their start and end apart: 4, of which 3 were waited for; matrix products, arithmetic and copies ran while one was open for 9% of the time, Pallas kernels for 4%

profile of v2, /device:TPU:1, one launch (start us, length us, event | category | flops | bytes accessed | tf_op | source)
XLA Modules:
  0.0 382.2 jit_solution(12003471973569282977)
XLA Ops:
  6.5 0.0 all-gather.2.cloned.1.call-start
  6.5 0.0 copy-start.1
  6.5 0.0 copy-start.2
  6.5 4.7 %constant_dynamic-slice_fusion = bf16[992,2048]{1,0:T(8,128)(2,1)} fusion(bf16[992,3968]{1,0:T(8,128)(2,1)} %param.7, s32[]{:T(128)S(6)} %select_n.75), kind=kLoop, calls=%fused_computation.53 | loop fusion | bytes 8126468 | tf_op jit(solution)/shard_map/dynamic_slice | solution.py:90
  11.2 0.0 all-gather.2.cloned.1.call-update
  11.3 152.8 %all-gather.2.cloned.1.call-done = bf16[3968,2048]{1,0:T(8,128)(2,1)} async-done(((bf16[992,2048]{1,0:T(8,128)(2,1)}), bf16[3968,2048]{1,0:T(8,128)(2,1)}) %all-gather.2.cloned.1.call-update) | async-done | bytes 16252944 | tf_op jit(solution)/shard_map/all_gather | solution.py:91
  164.0 0.8 collective-permute-start
  164.9 0.0 copy-done.1
  164.9 0.0 copy-done.2
  164.9 1.2 reduce-window.6
  166.1 0.2 slice_reduce_fusion
  166.4 0.1 fusion.7
  166.5 2.4 scatter_custom_fusion
  168.9 0.7 all_to_all.24
  169.6 7.1 %all-to-all-start = ((s32[32,16,1]{1,2,0:T(1,128)}), s32[32,16,1]{1,2,0:T(1,128)S(1)}, u32[]{:S(2)}, u32[]{:S(2)}) async-start(s32[32,16,1]{1,2,0:T(1,128)} %bitcast.2), calls=%async_computation | async-start | bytes 32768 | tf_op jit(solution)/shard_map/all_to_all | solution.py:84
  176.7 6.6 %convolution_convert_fusion.3 = bf16[512,4096]{1,0:T(8,128)(2,1)} fusion(bf16[512,4096]{0,1:T(8,128)(2,1)} %bitcast.37, s32[512]{0:T(512)S(1)} %get-tuple-element.6), kind=kOutput, calls=%fused_computation.4 | convolution fusion | flops 2149842944 | bytes 8390656 | tf_op jit(solution)/shard_map/dot_general | solution.py:13
  183.3 6.0 %all-to-all-done = s32[32,16,1]{1,2,0:T(1,128)S(1)} async-done(((s32[32,16,1]{1,2,0:T(1,128)}), s32[32,16,1]{1,2,0:T(1,128)S(1)}, u32[]{:S(2)}, u32[]{:S(2)}) %all-to-all-start) | async-done | bytes 2080 | tf_op jit(solution)/shard_map/all_to_all | solution.py:84
  189.3 7.4 %all-to-all-start.1 = ((bf16[32,16,4096]{2,1,0:T(8,128)(2,1)}), bf16[32,16,4096]{2,1,0:T(8,128)(2,1)}, u32[]{:S(2)}, u32[]{:S(2)}) async-start(bf16[32,16,4096]{2,1,0:T(8,128)(2,1)} %bitcast.34), calls=%async_computation.1 | async-start | bytes 8388608 | tf_op jit(solution)/shard_map/all_to_all | solution.py:83
  196.7 0.5 broadcast.188
  197.3 0.7 reduce.5
  197.9 0.1 all_to_all.26
  198.0 50.8 %all-to-all-done.1 = bf16[32,16,4096]{2,1,0:T(8,128)(2,1)} async-done(((bf16[32,16,4096]{2,1,0:T(8,128)(2,1)}), bf16[32,16,4096]{2,1,0:T(8,128)(2,1)}, u32[]{:S(2)}, u32[]{:S(2)}) %all-to-all-start.1) | async-done | bytes 4194336 | tf_op jit(solution)/shard_map/all_to_all | solution.py:83
  248.8 6.4 %convolution_convert_fusion.4.x_ref = bf16[496,4096]{1,0:T(8,128)(2,1)} fusion(bf16[512,4096]{1,0:T(8,128)(2,1)} %bitcast.5, s32[512]{0:T(512)S(1)} %all_to_all.26), kind=kOutput, calls=%fused_computation.5 | convolution fusion | flops 2082660352 | bytes 8259584 | tf_op jit(solution)/shard_map/dot_general | solution.py:13
  255.2 9.2 %shard_map.46 = bf16[512,3968]{1,0:T(8,128)(2,1)} custom-call(bf16[496,4096]{1,0:T(8,128)(2,1)} %convolution_convert_fusion.4.x_ref), custom_call_target="tpu_custom_call" | custom-call | bytes 8126464 | tf_op jit(solution)/shard_map/pallas_call | solution.py:31
  264.5 14.4 %convolution_convert_fusion.6.x_ref = bf16[512,2048]{1,0:T(8,128)(2,1)} fusion(bf16[512,3968]{1,0:T(8,128)(2,1)} %shard_map.46, bf16[3968,2048]{1,0:T(8,128)(2,1)} %all-gather.2.cloned.1.call-done), kind=kOutput, calls=%fused_computation.8 | convolution fusion | flops 8322547712 | bytes 22413312 | tf_op jit(solution)/shard_map/dot_general | solution.py:103
  278.9 4.7 %shard_map.47 = bf16[256,4096]{1,0:T(8,128)(2,1)} custom-call(bf16[512,2048]{1,0:T(8,128)(2,1)} %convolution_convert_fusion.6.x_ref), custom_call_target="tpu_custom_call" | custom-call | bytes 4194304 | tf_op jit(solution)/shard_map/pallas_call | solution.py:51
  283.6 0.0 collective-permute-done
  283.6 14.4 %convolution_convert_fusion.5.x_ref = bf16[512,2048]{1,0:T(8,128)(2,1)} fusion(bf16[512,3968]{1,0:T(8,128)(2,1)} %shard_map.46, bf16[3968,2048]{1,0:T(8,128)(2,1)} %collective-permute-done), kind=kOutput, calls=%fused_computation.7 | convolution fusion | flops 8322547712 | bytes 22413312 | tf_op jit(solution)/shard_map/dot_general | solution.py:105
  298.0 4.7 %shard_map.48 = bf16[256,4096]{1,0:T(8,128)(2,1)} custom-call(bf16[512,2048]{1,0:T(8,128)(2,1)} %convolution_convert_fusion.5.x_ref), custom_call_target="tpu_custom_call" | custom-call | bytes 4194304 | tf_op jit(solution)/shard_map/pallas_call | solution.py:51
  302.7 0.0 copy-start
  302.7 3.0 convolution_convert_fusion.1
  305.8 0.0 copy-done
  305.8 1.4 fusion
  307.1 57.4 %all_to_all.36 = bf16[32,16,4096]{2,1,0:T(8,128)(2,1)S(1)} all-to-all(bf16[32,16,4096]{2,1,0:T(8,128)(2,1)S(1)} %bitcast.33), channel_id=1, replica_groups=mesh['grp'=4,'tile'=32] {'tile'}, dimensions={0} | all-to-all | bytes 8388608 | tf_op jit(solution)/shard_map/all_to_all | solution.py:108
  364.6 4.3 %convolution_convert_fusion = bf16[512,4096]{1,0:T(8,128)(2,1)} fusion(bf16[512,4096]{1,0:T(8,128)(2,1)S(1)} %bitcast.35, s32[512]{0:T(512)S(1)} %get-tuple-element.6), kind=kOutput, calls=%fused_computation.1 | convolution fusion | flops 2149842944 | bytes 8390656 | tf_op jit(solution)/shard_map/dot_general | solution.py:110
  368.9 6.4 %copy.10 = bf16[512,4096]{0,1:T(8,128)(2,1)} copy(bf16[512,4096]{1,0:T(8,128)(2,1)} %convolution_convert_fusion) | data formatting | bytes 8388608 | tf_op jit(solution)/shard_map/convert_element_type | solution.py:110
  (6 shorter events, 0.1 us)
Async XLA Ops:
  6.5 157.5 %all-gather.2.cloned.1.call-start = ((), (), s32[]{:S(2)}) async-start(), calls=%async_computation.3 | async-start | bytes 20316160 | tf_op jit(solution)/shard_map/all_gather | solution.py:91
  6.5 158.4 %copy-start.1 = (s32[512]{0:T(512)S(1)}, s32[512]{0:T(512)}, u32[]{:S(2)}) copy-start(s32[512]{0:T(512)} %param.5) | copy-start | bytes 6148
  6.5 158.4 %copy-start.2 = (s32[512]{0:T(512)S(1)}, s32[512]{0:T(512)}, u32[]{:S(2)}) copy-start(s32[512]{0:T(512)} %param.6) | copy-start | bytes 6148
  164.0 119.6 %collective-permute-start = (bf16[3968,2048]{1,0:T(8,128)(2,1)}, bf16[3968,2048]{1,0:T(8,128)(2,1)}, u32[]{:S(2)}, u32[]{:S(2)}) collective-permute-start(bf16[3968,2048]{1,0:T(8,128)(2,1)} %all-gather.2.cloned.1.call-done), channel_id=1, source_target_pairs={{0,1},{1,0},{2,3},{3,2},{4,5},{5,4},{6,7},{7,6},{8,9},{9,8},{10,11... | collective-permute-start | bytes 48758792 | tf_op jit(solution)/shard_map/ppermute | solution.py:92
  169.6 19.7 %all-to-all-start = ((s32[32,16,1]{1,2,0:T(1,128)}), s32[32,16,1]{1,2,0:T(1,128)S(1)}, u32[]{:S(2)}, u32[]{:S(2)}) async-start(s32[32,16,1]{1,2,0:T(1,128)} %bitcast.2), calls=%async_computation | async-start | bytes 32768 | tf_op jit(solution)/shard_map/all_to_all | solution.py:84
  189.3 59.5 %all-to-all-start.1 = ((bf16[32,16,4096]{2,1,0:T(8,128)(2,1)}), bf16[32,16,4096]{2,1,0:T(8,128)(2,1)}, u32[]{:S(2)}, u32[]{:S(2)}) async-start(bf16[32,16,4096]{2,1,0:T(8,128)(2,1)} %bitcast.34), calls=%async_computation.1 | async-start | bytes 8388608 | tf_op jit(solution)/shard_map/all_to_all | solution.py:83
  302.7 3.0 copy-start
Sparse Core Ops, SparseCore 0:
  11.4 152.6 all-gather.1

commit v3 on v2

--- a/solution.py
+++ b/solution.py
@@ -6,6 +6,7 @@
 from jax.experimental.pallas import tpu as pltpu
 
 ROWT_DEV = 8
+PLANE = 4
 
 
 def pick_rows(index, count, data):
@@ -84,27 +85,59 @@
         lax.all_to_all(send_ids, "tile", split_axis=0, concat_axis=0, tiled=True),
     )
     dense = tiles_to_rows(pick_rows(recv_ids, per_dest, recv_tiles), ROWT_DEV, edge)
-    core = lax.axis_index("tile") % 2
-    span = (width // 2 + 127) // 128 * 128
-    shift = (width - span) // edge
-    mine = lax.dynamic_slice_in_dim(cycle_panel, core * (width - span), span, axis=1)
-    gathered = lax.all_gather(mine, "grp", axis=0, tiled=True)
-    partner = lax.ppermute(gathered, "tile", [(i, i ^ 1) for i in range(parts)])
-    half = span // edge
+    tile = lax.axis_index("tile")
+    core = tile % 2
+    chip = tile // 2
+    side = PLANE
+    cx = chip // side
+    cz = chip % side
+    colour = (cx + cz) % 2
+    quarter = 1024
+    nq = 4
+    qt = quarter // edge
+    base = [min(q * quarter, width - quarter) for q in range(nq)]
+    mine_q = 2 * colour + core
+    start_col = jnp.where(mine_q == nq - 1, base[nq - 1], mine_q * quarter)
+    mine = lax.dynamic_slice_in_dim(cycle_panel, start_col, quarter, axis=1)
+    own = lax.all_gather(mine, "grp", axis=0, tiled=True)
+    pair = [(i, i ^ 1) for i in range(parts)]
+
+    def device(x, z, k):
+        return ((x % side) * side + (z % side)) * 2 + k
+
+    moves = []
+    for dx, dz in ((-1, 0), (1, 0), (0, -1), (0, 1)):
+        moves.append(
+            [
+                (device(x, z, k), device(x + dx, z + dz, k))
+                for x in range(side)
+                for z in range(side)
+                for k in range(2)
+            ]
+        )
+    rows_b = own.shape[0] // 4
+    from_partner = lax.ppermute(own, "tile", pair)
+    received = []
+    for b, perm in enumerate(moves):
+        received.append(lax.ppermute(own[b * rows_b : (b + 1) * rows_b], "tile", perm))
     valid = recv_ids < per_dest
     row_t = recv_ids // nvt
     col_t = recv_ids % nvt
-    col_mine = col_t - core * shift
-    in_mine = valid & (col_mine >= 0) & (col_mine < half)
-    col_partner = col_t - (1 - core) * shift
-    in_partner = valid & ~in_mine
-    idx_mine = jnp.where(in_mine, row_t * half + col_mine, ROWT_DEV * half)
-    idx_partner = jnp.where(in_partner, row_t * half + col_partner, ROWT_DEV * half)
-    out_mine = jnp.dot(dense, gathered, preferred_element_type=jnp.float32).astype(jnp.bfloat16)
-    ans_mine = take_rows(idx_mine, rows_to_tiles(out_mine, edge))
-    out_partner = jnp.dot(dense, partner, preferred_element_type=jnp.float32).astype(jnp.bfloat16)
-    ans_partner = take_rows(idx_partner, rows_to_tiles(out_partner, edge))
-    answer = ans_mine + ans_partner
+    col_q = jnp.minimum(col_t // qt, nq - 1)
+    unused = ROWT_DEV * qt
+
+    def answer_part(panel_q, q):
+        qbase = jnp.where(q == nq - 1, base[nq - 1] // edge, q * qt)
+        idx = jnp.where(valid & (col_q == q), row_t * qt + col_t - qbase, unused)
+        out = jnp.dot(dense, panel_q, preferred_element_type=jnp.float32).astype(jnp.bfloat16)
+        return take_rows(idx, rows_to_tiles(out, edge))
+
+    answer = answer_part(own, mine_q)
+    answer = answer + answer_part(from_partner, 2 * colour + 1 - core)
+    from_x = jnp.concatenate(received, axis=0)
+    from_partner_x = lax.ppermute(from_x, "tile", pair)
+    answer = answer + answer_part(from_x, 2 * (1 - colour) + core)
+    answer = answer + answer_part(from_partner_x, 2 * (1 - colour) + 1 - core)
     returned = lax.all_to_all(answer, "tile", split_axis=0, concat_axis=0, tiled=True)
     onehot_back = (position[None, :] == jnp.arange(parts * capacity)[:, None]).astype(returned.dtype)
     result_t = jnp.dot(returned.T, onehot_back, preferred_element_type=jnp.float32).astype(returned.dtype)

time: 383 us -> 371 us (0.969); the launches traced: 382 us -> 364 us
  waiting for transfers between devices: 210 us -> 153 us
  matrix products: 50.6 us -> 64.6 us
  local copies, waits for them, and re-layouts: 15.1 us -> 28.9 us
  starting transfers between devices: 15.4 us -> 23.8 us
  Pallas kernels: 18.6 us -> 23 us
    all_gather x1, waiting for transfers between devices: 153 us -> 69.9 us  [layer(): own = lax.all_gather(mine, 'grp', axis=0, tiled=True)]
    ppermute x1 -> x6, waiting for transfers between devices: 0.01 us -> 82.7 us  [the longest x4 82.7 us: layer(): lax.ppermute(own[b * rows_b:(b + 1) * rows_b], 'tile', perm)]
    all_to_all x1, waiting for transfers between devices: 50.8 us -> 0.01 us  [layer(): lax.all_to_all(send_tiles, 'tile', split_axis=0, concat_axis=0, tiled=True)]
    dot_general x2 -> x4, matrix products: 28.9 us -> 38.4 us  [answer_part(): jnp.dot(dense, panel_q, preferred_element_type=jnp.float32)]
    ppermute x1 -> x6, starting transfers between devices: 0.84 us -> 9.31 us  [the longest x4 6.5 us: layer(): lax.ppermute(own[b * rows_b:(b + 1) * rows_b], 'tile', perm)]
    unnamed x6 -> x15, local copies, waits for them, and re-layouts: 0.01 us -> 7.65 us
    dot_general x2 -> x4, matrix products: 4.4 us -> 11 us  [take_rows(): jnp.dot(onehot, data, preferred_element_type=jnp.float32).astype(data.dtype)]
    slice x1 -> x2, local copies, waits for them, and re-layouts: 0.22 us -> 6.61 us  [the longest x1 6.39 us: layer(): own[b * rows_b:(b + 1) * rows_b]]
  transfers between devices with their start and end apart: 4 -> 9, of which waited for: 3 -> 4; matrix products, arithmetic and copies ran while one was open for 9% -> 19% of each run, Pallas kernels for 4% -> 5%
where the time goes in v3:
time: 371 us; the launch traced here: 364 us
  waiting for transfers between devices  153 us (41%)
  matrix products  64.6 us (17%)
  blocking collectives  55.3 us (15%)
  local copies, waits for them, and re-layouts  28.9 us (8%)
  starting transfers between devices  23.8 us (6%)
  Pallas kernels  23 us (6%)
  between operations  13.8 us (4%)
    ppermute x4, waiting for transfers between devices, layer(): lax.ppermute(own[b * rows_b:(b + 1) * rows_b], 'tile', perm)  82.7 us
    all_gather x1, waiting for transfers between devices, layer(): own = lax.all_gather(mine, 'grp', axis=0, tiled=True)  69.9 us
    all_to_all x1, blocking collectives, layer(): lax.all_to_all(answer, 'tile', split_axis=0, concat_axis=0, tiled=True)  55.3 us
    dot_general x4, matrix products, answer_part(): jnp.dot(dense, panel_q, preferred_element_type=jnp.float32)  38.4 us
    pallas_call x4, Pallas kernels, rows_to_tiles(): pl.pallas_call(kernel, out_shape=jax.ShapeDtypeStruct((row_tiles * col_ti...  13.7 us
    dot_general x4, matrix products, take_rows(): jnp.dot(onehot, data, preferred_element_type=jnp.float32).astype(data.dtype)  11 us
    dot_general x2, matrix products, pick_rows(): jnp.dot(onehot, data, preferred_element_type=jnp.float32).astype(data.dtype)  10.9 us
    all_to_all x1, starting transfers between devices, layer(): lax.all_to_all(send_ids, 'tile', split_axis=0, concat_axis=0, tiled=True)  9.42 us
  transfers between devices with their start and end apart: 9, of which 4 were waited for; matrix products, arithmetic and copies ran while one was open for 19% of the time, Pallas kernels for 5%

profile of v3, /device:TPU:1, one launch (start us, length us, event | category | flops | bytes accessed | tf_op | source)
XLA Modules:
  0.0 364.0 jit_solution(9199623291459892892)
XLA Ops:
  6.5 3.0 constant_dynamic-slice_fusion
  9.6 0.0 all-gather.2.cloned.1.call-update
  9.7 1.2 reduce-window.6
  10.8 0.2 slice_reduce_fusion
  11.1 0.1 fusion.11
  11.2 2.4 scatter_custom_fusion
  13.7 0.7 all_to_all.24
  14.4 9.4 %all-to-all-start = ((s32[32,16,1]{1,2,0:T(1,128)}), s32[32,16,1]{1,2,0:T(1,128)S(1)}, u32[]{:S(2)}, u32[]{:S(2)}) async-start(s32[32,16,1]{1,2,0:T(1,128)} %bitcast.2), calls=%async_computation | async-start | bytes 32768 | tf_op jit(solution)/shard_map/all_to_all | solution.py:85
  23.8 69.9 %all-gather.2.cloned.1.call-done = bf16[3968,1024]{1,0:T(8,128)(2,1)} async-done(((bf16[992,1024]{1,0:T(8,128)(2,1)}), bf16[3968,1024]{1,0:T(8,128)(2,1)}) %all-gather.2.cloned.1.call-update) | async-done | bytes 8126480 | tf_op jit(solution)/shard_map/all_gather | solution.py:102
  93.7 6.4 %fusion.24 = (bf16[992,1024]{1,0:T(8,128)(2,1)}, bf16[992,1024]{1,0:T(8,128)(2,1)}, bf16[992,1024]{1,0:T(8,128)(2,1)}, bf16[992,1024]{1,0:T(8,128)(2,1)}) fusion(bf16[3968,1024]{1,0:T(8,128)(2,1)} %all-gather.2.cloned.1.call-done), kind=kLoop, calls=%fused_computation.77 | loop fusion | bytes 16252928 | tf_op jit(solution)/shard_map/slice | solution.py:122
  100.1 2.4 collective-permute-start.1
  102.5 0.0 collective-permute-start.2
  102.5 2.7 collective-permute-start.3
  105.2 1.4 collective-permute-start
  106.6 4.4 %convolution_convert_fusion.5 = bf16[512,4096]{1,0:T(8,128)(2,1)} fusion(bf16[512,4096]{0,1:T(8,128)(2,1)S(1)} %bitcast.43, s32[512]{0:T(512)S(1)} %get-tuple-element.10), kind=kOutput, calls=%fused_computation.6 | convolution fusion | flops 2149842944 | bytes 8390656 | tf_op jit(solution)/shard_map/dot_general | solution.py:14
  111.0 0.0 all-to-all-done
  111.0 5.0 %all-to-all-start.1 = ((bf16[32,16,4096]{2,1,0:T(8,128)(2,1)}), bf16[32,16,4096]{2,1,0:T(8,128)(2,1)}, u32[]{:S(2)}, u32[]{:S(2)}) async-start(bf16[32,16,4096]{2,1,0:T(8,128)(2,1)} %bitcast.40), calls=%async_computation.1 | async-start | bytes 8388608 | tf_op jit(solution)/shard_map/all_to_all | solution.py:84
  116.1 1.4 collective-permute-start.4
  117.5 28.1 %collective-permute-done.1 = bf16[992,1024]{1,0:T(8,128)(2,1)} collective-permute-done((bf16[992,1024]{1,0:T(8,128)(2,1)}, bf16[992,1024]{1,0:T(8,128)(2,1)}, u32[]{:S(2)}, u32[]{:S(2)}) %collective-permute-start.1) | collective-permute-done | bytes 2031648 | tf_op jit(solution)/shard_map/ppermute | solution.py:122
  145.6 3.1 constant_dynamic-update-slice_fusion.3
  148.7 0.0 collective-permute-done.2
  148.7 3.0 constant_dynamic-update-slice_fusion.2
  151.7 0.4 collective-permute-done.3
  152.2 1.5 constant_dynamic-update-slice_fusion.1
  153.7 54.2 %collective-permute-done.4 = bf16[992,1024]{1,0:T(8,128)(2,1)S(1)} collective-permute-done((bf16[992,1024]{1,0:T(8,128)(2,1)}, bf16[992,1024]{1,0:T(8,128)(2,1)S(1)}, u32[]{:S(2)}, u32[]{:S(2)}) %collective-permute-start.4) | collective-permute-done | bytes 2031648 | tf_op jit(solution)/shard_map/ppermute | solution.py:122
  207.8 1.5 constant_dynamic-update-slice_fusion
  209.3 1.4 collective-permute-start.5
  210.7 0.5 broadcast.352
  211.2 0.7 reduce.5
  211.9 0.1 all_to_all.26
  212.0 6.4 %convolution_convert_fusion.6.x_ref = bf16[496,4096]{1,0:T(8,128)(2,1)} fusion(bf16[512,4096]{1,0:T(8,128)(2,1)} %bitcast.5, s32[512]{0:T(512)S(1)} %all_to_all.26), kind=kOutput, calls=%fused_computation.7 | convolution fusion | flops 2082660352 | bytes 8259584 | tf_op jit(solution)/shard_map/dot_general | solution.py:14
  218.5 9.3 %shard_map.46 = bf16[512,3968]{1,0:T(8,128)(2,1)} custom-call(bf16[496,4096]{1,0:T(8,128)(2,1)} %convolution_convert_fusion.6.x_ref), custom_call_target="tpu_custom_call" | custom-call | bytes 8126464 | tf_op jit(solution)/shard_map/pallas_call | solution.py:32
  227.8 10.0 %convolution_convert_fusion.10.x_ref = bf16[512,1024]{1,0:T(8,128)(2,1)} fusion(bf16[512,3968]{1,0:T(8,128)(2,1)} %shard_map.46, bf16[3968,1024]{1,0:T(8,128)(2,1)} %all-gather.2.cloned.1.call-done), kind=kOutput, calls=%fused_computation.14 | convolution fusion | flops 4161273856 | bytes 13238272 | tf_op jit(solution)/shard_map/dot_general | solution.py:132
  237.8 3.4 shard_map.47
  241.2 10.2 %convolution_convert_fusion.8.x_ref = bf16[512,1024]{1,0:T(8,128)(2,1)} fusion(bf16[512,3968]{1,0:T(8,128)(2,1)} %shard_map.46, bf16[3968,1024]{1,0:T(8,128)(2,1)} %constant_dynamic-update-slice_fusion), kind=kOutput, calls=%fused_computation.12 | convolution fusion | flops 4161273856 | bytes 13238272 | tf_op jit(solution)/shard_map/dot_general | solution.py:132
  251.4 3.4 shard_map.49
  254.8 0.0 collective-permute-done
  254.8 10.0 %convolution_convert_fusion.9.x_ref = bf16[512,1024]{1,0:T(8,128)(2,1)} fusion(bf16[512,3968]{1,0:T(8,128)(2,1)} %shard_map.46, bf16[3968,1024]{1,0:T(8,128)(2,1)} %collective-permute-done), kind=kOutput, calls=%fused_computation.13 | convolution fusion | flops 4161273856 | bytes 13238272 | tf_op jit(solution)/shard_map/dot_general | solution.py:132
  264.8 3.4 shard_map.48
  268.2 2.6 convolution_convert_fusion.2
  270.8 1.3 fusion
  272.1 3.3 fusion.1
  275.4 8.2 %convolution_convert_fusion.7.x_ref = bf16[512,1024]{1,0:T(8,128)(2,1)} fusion(bf16[512,3968]{1,0:T(8,128)(2,1)S(1)} %copy-done.2, bf16[3968,1024]{1,0:T(8,128)(2,1)} %collective-permute-done.5), kind=kOutput, calls=%fused_computation.11 | convolution fusion | flops 4161273856 | bytes 13238272 | tf_op jit(solution)/shard_map/dot_general | solution.py:132
  283.6 3.4 shard_map.50
  287.1 3.8 %fusion.2 = bf16[512,4096]{1,0:T(8,128)(2,1)S(1)} fusion(bf16[512,4096]{1,0:T(8,128)(2,1)} %fusion.1, bf16[128,4096]{1,0:T(8,128)(2,1)} %shard_map.50, s32[512]{0:T(512)S(1)} %get-tuple-element.5), kind=kOutput, calls=%fused_computation.10 | convolution fusion | flops 541130752 | bytes 9439232 | tf_op jit(solution)/shard_map/dot_general | solution.py:19
  290.9 55.3 %all_to_all.36 = bf16[32,16,4096]{2,1,0:T(8,128)(2,1)S(1)} all-to-all(bf16[32,16,4096]{2,1,0:T(8,128)(2,1)S(1)} %bitcast.39), channel_id=1, replica_groups=mesh['grp'=4,'tile'=32] {'tile'}, dimensions={0} | all-to-all | bytes 8388608 | tf_op jit(solution)/shard_map/all_to_all | solution.py:141
  346.2 4.3 %convolution_convert_fusion.4 = bf16[512,4096]{1,0:T(8,128)(2,1)} fusion(bf16[512,4096]{1,0:T(8,128)(2,1)S(1)} %bitcast.41, s32[512]{0:T(512)S(1)} %get-tuple-element.10), kind=kOutput, calls=%fused_computation.5 | convolution fusion | flops 2149842944 | bytes 8390656 | tf_op jit(solution)/shard_map/dot_general | solution.py:143
  350.5 6.4 %copy.10 = bf16[512,4096]{0,1:T(8,128)(2,1)} copy(bf16[512,4096]{1,0:T(8,128)(2,1)} %convolution_convert_fusion.4) | data formatting | bytes 8388608 | tf_op jit(solution)/shard_map/convert_element_type | solution.py:143
  (22 shorter events, 0.1 us)
Async XLA Ops:
  6.5 3.1 copy-start.4
  6.5 3.1 copy-start.3
  6.5 87.2 %all-gather.2.cloned.1.call-start = ((), (), s32[]{:S(2)}) async-start(), calls=%async_computation.3 | async-start | bytes 10158080 | tf_op jit(solution)/shard_map/all_gather | solution.py:102
  14.4 96.7 %all-to-all-start = ((s32[32,16,1]{1,2,0:T(1,128)}), s32[32,16,1]{1,2,0:T(1,128)S(1)}, u32[]{:S(2)}, u32[]{:S(2)}) async-start(s32[32,16,1]{1,2,0:T(1,128)} %bitcast.2), calls=%async_computation | async-start | bytes 32768 | tf_op jit(solution)/shard_map/all_to_all | solution.py:85
  93.7 12.9 %copy-start.5 = (bf16[512,64,64]{0,2,1:T(8,128)(2,1)S(1)}, bf16[512,64,64]{0,2,1:T(8,128)(2,1)}, u32[]{:S(2)}) copy-start(bf16[512,64,64]{0,2,1:T(8,128)(2,1)} %param.4) | copy-start | bytes 12582916
  100.1 45.5 %collective-permute-start.1 = (bf16[992,1024]{1,0:T(8,128)(2,1)}, bf16[992,1024]{1,0:T(8,128)(2,1)}, u32[]{:S(2)}, u32[]{:S(2)}) collective-permute-start(bf16[992,1024]{1,0:T(8,128)(2,1)} %get-tuple-element.14), channel_id=1, source_target_pairs={{0,24},{1,25},{2,26},{3,27},{4,28},{5,29},{6,30},{7,31},{8,0},{9,1... | collective-permute-start | bytes 6094856 | tf_op jit(solution)/shard_map/ppermute | solution.py:122
  102.5 46.2 %collective-permute-start.2 = (bf16[992,1024]{1,0:T(8,128)(2,1)}, bf16[992,1024]{1,0:T(8,128)(2,1)}, u32[]{:S(2)}, u32[]{:S(2)}) collective-permute-start(bf16[992,1024]{1,0:T(8,128)(2,1)} %get-tuple-element.13), channel_id=1, source_target_pairs={{0,8},{1,9},{2,10},{3,11},{4,12},{5,13},{6,14},{7,15},{8,16},{9,17... | collective-permute-start | bytes 6094856 | tf_op jit(solution)/shard_map/ppermute | solution.py:122
  102.5 49.6 %collective-permute-start.3 = (bf16[992,1024]{1,0:T(8,128)(2,1)}, bf16[992,1024]{1,0:T(8,128)(2,1)S(1)}, u32[]{:S(2)}, u32[]{:S(2)}) collective-permute-start(bf16[992,1024]{1,0:T(8,128)(2,1)} %get-tuple-element.12), channel_id=1, source_target_pairs={{0,6},{1,7},{2,0},{3,1},{4,2},{5,3},{6,4},{7,5},{8,14},{9,15},{10,... | collective-permute-start | bytes 6094856 | tf_op jit(solution)/shard_map/ppermute | solution.py:122
  105.2 149.6 %collective-permute-start = (bf16[3968,1024]{1,0:T(8,128)(2,1)}, bf16[3968,1024]{1,0:T(8,128)(2,1)}, u32[]{:S(2)}, u32[]{:S(2)}) collective-permute-start(bf16[3968,1024]{1,0:T(8,128)(2,1)} %all-gather.2.cloned.1.call-done), channel_id=1, source_target_pairs={{0,1},{1,0},{2,3},{3,2},{4,5},{5,4},{6,7},{7,6},{8,9},{9,8},{10,11... | collective-permute-start | bytes 24379400 | tf_op jit(solution)/shard_map/ppermute | solution.py:119
  111.0 101.0 %all-to-all-start.1 = ((bf16[32,16,4096]{2,1,0:T(8,128)(2,1)}), bf16[32,16,4096]{2,1,0:T(8,128)(2,1)}, u32[]{:S(2)}, u32[]{:S(2)}) async-start(bf16[32,16,4096]{2,1,0:T(8,128)(2,1)} %bitcast.40), calls=%async_computation.1 | async-start | bytes 8388608 | tf_op jit(solution)/shard_map/all_to_all | solution.py:84
  116.1 91.8 %collective-permute-start.4 = (bf16[992,1024]{1,0:T(8,128)(2,1)}, bf16[992,1024]{1,0:T(8,128)(2,1)S(1)}, u32[]{:S(2)}, u32[]{:S(2)}) collective-permute-start(bf16[992,1024]{1,0:T(8,128)(2,1)} %get-tuple-element.11), channel_id=1, source_target_pairs={{0,2},{1,3},{2,4},{3,5},{4,6},{5,7},{6,0},{7,1},{8,10},{9,11},{10,... | collective-permute-start | bytes 6094856 | tf_op jit(solution)/shard_map/ppermute | solution.py:122
  209.3 66.1 %collective-permute-start.5 = (bf16[3968,1024]{1,0:T(8,128)(2,1)}, bf16[3968,1024]{1,0:T(8,128)(2,1)}, u32[]{:S(2)}, u32[]{:S(2)}) collective-permute-start(bf16[3968,1024]{1,0:T(8,128)(2,1)} %constant_dynamic-update-slice_fusion), channel_id=1, source_target_pairs={{0,1},{1,0},{2,3},{3,2},{4,5},{5,4},{6,7},{7,6},{8,9},{9,8},{10,11... | collective-permute-start | bytes 24379400 | tf_op jit(solution)/shard_map/ppermute | solution.py:138
  268.2 2.6 copy-start.1
  270.8 1.3 copy-start
  272.1 3.3 copy-start.2
Sparse Core Ops, SparseCore 0:
  9.7 83.9 all-gather.1
